TPU v7x, 128 devices: a whole 4x4x4 slice. The times are simulated.
128 devices in a mesh: req: 32 (over x, z, core), seq: 4 (over y).
Axes of the slice: x: 4, y: 4, z: 4, core: 2. Of those that a mesh axis runs over, the one named last changes fastest.
Arguments:
- xs: bfloat16 [16384, 8192], P(('req', 'seq')), may hold values from -6 to 6
- bc: bfloat16 [16384, 2048], P(('req', 'seq')), may hold values from -6 to 6
- zgate: bfloat16 [16384, 8192], P(('req', 'seq'))
- dt_raw: bfloat16 [16384, 128], P(('req', 'seq'))
- dt_bias: float32 [128], replicated
- a_log: float32 [128], replicated, may hold values from -0.5 to 1
- d_skip: float32 [128], replicated, may hold values from 0.5 to 1.5
- norm_gain: float32 [8192], replicated, may hold values from 0.1 to 1.9
- resid: bfloat16 [16384, 4096], P('req', 'seq')
- w_out: bfloat16 [8192, 4096], P('req'), may hold values from -0.0625 to 0.0625
- final_gain: float32 [4096], replicated, may hold values from 0.1 to 1.9
- head_weight: bfloat16 [4096, 32768], P(None, ('req', 'seq')), may hold values from -0.09375 to 0.09375
- lengths: int32 [32, 2], P('req'), may hold values from 1 to 511, as said below
Outputs:
- layer_out: bfloat16 [16384, 4096], P('req', 'seq')
- logits: float32 [64, 32768], P(None, ('req', 'seq'))
Inputs may be any that keep to these rules, and one draw needn't show every extreme that they name: Every request has at least one row; a group's lengths sum to at most 512, and to exactly 512 in at least two groups, where one request takes all but 2 - 1 rows.
All inputs are finite; a program needn't handle non-finite values.
Results may differ from a plain program's by a relative error of at most 0.013.
Values may be sent and summed in bfloat16 or wider, within the bound.
No kernel may reach another device: no remote copies, remote signals or barrier semaphores. Data moves between devices by JAX's collectives and lax.ppermute only.
A program may use at most 128 MiB of HBM per device.

v0:
```python
import jax
import jax.numpy as jnp
from jax import lax
from jax.sharding import PartitionSpec as P

SSM_CHANNEL_COUNT = 128
HEAD_DIM = 64
NGROUPS = 8
STATE = 128


def split_halves(value):
    upper = value.astype(jnp.bfloat16)
    lower = (value - upper.astype(jnp.float32)).astype(jnp.bfloat16)
    return (upper, lower)


def group_inner(operands):
    cum_g, scores_g, inflow_g, x_g, allowed_mask = operands
    diff = cum_g[:, None, :] - cum_g[None, :, :]
    decay = jnp.where(allowed_mask[:, :, None], jnp.exp(jnp.minimum(diff, 0.0)), 0.0)
    weights = decay * scores_g[:, :, None] * inflow_g[None, :, :]
    upper, lower = split_halves(weights)
    first_part = jnp.einsum("tsk,skp->tkp", upper, x_g, preferred_element_type=jnp.float32)
    second_part = jnp.einsum("tsk,skp->tkp", lower, x_g, preferred_element_type=jnp.float32)
    return first_part + second_part


def block_terms(xb, bb, cb, dtb, segment, live, prev_seg, rate, d_skip, groups):
    rows = xb.shape[0]
    heads = rate.shape[0]
    per_group = heads // groups
    x4 = xb.reshape(rows, groups, per_group, HEAD_DIM)
    bmat = bb.reshape(rows, groups, STATE)
    cmat = cb.reshape(rows, groups, STATE)
    livef = live.astype(jnp.float32)
    cum = jnp.cumsum(-rate[None, :] * dtb, axis=0)
    inflow = dtb * livef[:, None]
    index = jnp.arange(rows, dtype=jnp.int32)
    allowed_mask = (segment[:, None] == segment[None, :]) & (index[:, None] >= index[None, :])
    scores = jnp.einsum("tgn,sgn->gts", cmat, bmat, preferred_element_type=jnp.float32)
    cum_g = cum.reshape(rows, groups, per_group).transpose(1, 0, 2)
    inflow_g = inflow.reshape(rows, groups, per_group).transpose(1, 0, 2)
    x_g = x4.transpose(1, 0, 2, 3)
    allowed_all = jnp.broadcast_to(allowed_mask[None], (groups, rows, rows))
    y_groups = lax.map(group_inner, (cum_g, scores, inflow_g, x_g, allowed_all))
    y_inner = y_groups.transpose(1, 0, 2, 3)
    skip = d_skip.reshape(1, groups, per_group, 1) * x4.astype(jnp.float32)
    last_seg = segment[rows - 1]
    tail = (
        jnp.exp(cum[rows - 1][None, :] - cum)
        * (segment == last_seg).astype(jnp.float32)[:, None]
        * inflow
    )
    scaled = tail.reshape(rows, groups, per_group, 1) * x4.astype(jnp.float32)
    upper, lower = split_halves(scaled)
    state = jnp.einsum("sgkp,sgn->gkpn", upper, bmat, preferred_element_type=jnp.float32)
    state = state + jnp.einsum("sgkp,sgn->gkpn", lower, bmat, preferred_element_type=jnp.float32)
    keep = jnp.exp(cum[rows - 1]) * (last_seg == prev_seg).astype(jnp.float32)
    carry_w = jnp.exp(cum) * (segment == prev_seg).astype(jnp.float32)[:, None]
    return (y_inner + skip, keep, state.reshape(heads, HEAD_DIM, STATE), carry_w, cmat)


def carry_term(arriving_vector, cmat, carry_w, groups):
    rows = cmat.shape[0]
    heads = arriving_vector.shape[0]
    per_group = heads // groups
    state4 = arriving_vector.reshape(groups, per_group, HEAD_DIM, STATE)
    upper, lower = split_halves(state4)
    y_carry = jnp.einsum("tgn,gkpn->tgkp", cmat, upper, preferred_element_type=jnp.float32)
    y_carry = y_carry + jnp.einsum(
        "tgn,gkpn->tgkp", cmat, lower, preferred_element_type=jnp.float32
    )
    return y_carry * carry_w.reshape(rows, groups, per_group, 1)


def gate_norm(y, zgate, norm_gain, groups):
    rows = y.shape[0]
    gated = y * jax.nn.silu(zgate.astype(jnp.float32))
    blocks = gated.reshape(rows, groups, -1)
    meansq = jnp.mean(blocks * blocks, axis=-1, keepdims=True)
    normed = (blocks * lax.rsqrt(meansq + 1e-05)).reshape(rows, -1) * norm_gain[None, :]
    return normed.astype(jnp.bfloat16)


def on_device(
    xs,
    bc,
    zgate,
    dt_raw,
    dt_bias,
    a_log,
    d_skip,
    norm_gain,
    resid,
    w_out,
    final_gain,
    head_weight,
    lengths,
):
    rows = xs.shape[0]
    inner = xs.shape[1]
    seq_count = lax.axis_size("seq")
    place = lax.axis_index("seq")
    heads_all = a_log.shape[0]
    heads = heads_all // seq_count
    groups = NGROUPS // seq_count
    share = inner // seq_count
    bshare = groups * STATE
    group_rows = rows * seq_count
    bpart = bc[:, : NGROUPS * STATE].reshape(rows, seq_count, bshare)
    cpart = bc[:, NGROUPS * STATE :].reshape(rows, seq_count, bshare)
    packed = jnp.concatenate(
        [
            xs.reshape(rows, seq_count, share),
            zgate.reshape(rows, seq_count, share),
            bpart,
            cpart,
            dt_raw.reshape(rows, seq_count, heads),
        ],
        axis=2,
    )
    moved = lax.all_to_all(packed, "seq", split_axis=1, concat_axis=0, tiled=True)
    moved = moved.reshape(group_rows, -1)
    xg = moved[:, :share]
    zg = moved[:, share : 2 * share]
    bg = moved[:, 2 * share : 2 * share + bshare]
    cg = moved[:, 2 * share + bshare : 2 * share + 2 * bshare]
    dg = moved[:, 2 * share + 2 * bshare :]
    my_heads = lambda v: lax.dynamic_slice_in_dim(v, place * heads, heads)
    rate = jnp.exp(my_heads(a_log))
    skipw = my_heads(d_skip)
    steps_dt = jax.nn.softplus(dg.astype(jnp.float32) + my_heads(dt_bias)[None, :])
    lens = lengths[0]
    slots = lens.shape[0]
    ends = jnp.cumsum(lens)
    positions = jnp.arange(group_rows, dtype=jnp.int32)
    segment = jnp.sum((positions[:, None] >= ends[None, :]).astype(jnp.int32), axis=1)
    live = segment < slots
    state_in = jnp.zeros((heads, HEAD_DIM, STATE), jnp.float32)
    prev_seg = jnp.array(-1, jnp.int32)
    ys = []
    for chunk in range(seq_count):
        lo, hi = (chunk * rows, (chunk + 1) * rows)
        local, keep, state, carry_w, cmat = block_terms(
            xg[lo:hi],
            bg[lo:hi],
            cg[lo:hi],
            steps_dt[lo:hi],
            segment[lo:hi],
            live[lo:hi],
            prev_seg,
            rate,
            skipw,
            groups,
        )
        y4 = (local + carry_term(state_in, cmat, carry_w, groups)) * live[lo:hi].astype(
            jnp.float32
        )[:, None, None, None]
        ys.append(y4.reshape(rows, share))
        state_in = keep[:, None, None] * state_in + state
        prev_seg = segment[hi - 1]
    y = jnp.concatenate(ys, axis=0)
    gain = lax.dynamic_slice_in_dim(norm_gain, place * share, share)
    gated = gate_norm(y, zg, gain, groups)
    width = resid.shape[1]
    w_cols = lax.dynamic_slice_in_dim(w_out, place * width, width, axis=1)
    w_full = lax.all_gather(w_cols, "req", axis=0, tiled=True)
    gated_all = lax.all_gather(gated, "seq", axis=1, tiled=True)
    mixer = jnp.dot(gated_all, w_full, preferred_element_type=jnp.float32).astype(jnp.bfloat16)
    layer_out = (resid.astype(jnp.float32) + mixer.astype(jnp.float32)).astype(jnp.bfloat16)
    group_pos = jnp.arange(group_rows, dtype=jnp.int32)
    picker = (group_pos[None, :] == (ends - 1)[:, None]).astype(jnp.bfloat16)
    picked_rows = jnp.dot(picker, layer_out, preferred_element_type=jnp.float32).astype(
        jnp.bfloat16
    )
    collected = lax.all_gather(picked_rows, ("req", "seq"), axis=0, tiled=True)
    owners_all = collected.shape[0] // (seq_count * slots)
    last_rows = collected.reshape(owners_all, seq_count, slots, width).transpose(0, 2, 1, 3)
    last_rows = last_rows.reshape(owners_all * slots, seq_count * width).astype(jnp.float32)
    meansq = jnp.mean(last_rows * last_rows, axis=-1, keepdims=True)
    normed = (last_rows * lax.rsqrt(meansq + 1e-05) * final_gain[None, :]).astype(jnp.bfloat16)
    logits = jnp.dot(normed, head_weight, preferred_element_type=jnp.float32)
    return (layer_out, logits)


def solution(mesh):
    placed = (
        P(("req", "seq"), None),
        P(("req", "seq"), None),
        P(("req", "seq"), None),
        P(("req", "seq"), None),
        P(),
        P(),
        P(),
        P(),
        P("req", "seq"),
        P("req", None),
        P(),
        P(None, ("req", "seq")),
        P("req", None),
    )
    return jax.shard_map(
        on_device,
        mesh=mesh,
        in_specs=placed,
        out_specs=(P("req", "seq"), P(None, ("req", "seq"))),
        check_vma=False,
    )
```

profile of v0, /device:TPU:0, one launch (start us, length us, event | category | flops | bytes accessed | tf_op | source)
XLA Modules:
  0.0 426.5 jit_solution(4121959781990282691)
XLA Ops:
  8.6 4.1 copy.339
  12.6 3.3 constant_dynamic-update-slice_fusion.4
  16.0 4.1 copy.340
  20.3 3.3 constant_dynamic-update-slice_fusion.3
  25.7 5.1 %all-to-all-start = ((bf16[128,4,4640]{0,2,1:T(8,128)(2,1)}), bf16[128,4,4640]{0,2,1:T(8,128)(2,1)}, u32[]{:S(2)}, u32[]{:S(2)}) async-start(bf16[128,4,4640]{0,2,1:T(8,128)(2,1)} %constant_dynamic-update-slice_fusion), calls=%async_computation | async-start | bytes 9502720 | tf_op jit(solution)/shard_map/all_to_all | solution.py:123
  36.4 2.5 compare_convert_fusion.7
  40.3 45.8 %all-to-all-done = bf16[128,4,4640]{0,2,1:T(8,128)(2,1)} async-done(((bf16[128,4,4640]{0,2,1:T(8,128)(2,1)}), bf16[128,4,4640]{0,2,1:T(8,128)(2,1)}, u32[]{:S(2)}, u32[]{:S(2)}) %all-to-all-start) | async-done | bytes 4751392 | tf_op jit(solution)/shard_map/all_to_all | solution.py:123
  86.0 18.4 %copy.344 = bf16[4,128,1,4640]{1,0,3,2:T(4,128)(2,1)S(1)} copy(bf16[4,128,1,4640]{1,3,0,2:T(8,128)(2,1)} %bitcast.34) | data formatting | bytes 9502720 | tf_op jit(solution)/shard_map/all_to_all | solution.py:123
  106.2 1.8 fusion.157
  124.2 6.7 %while.40 = (s32[]{:T(128)}, f32[2,128,16,64]{1,3,2,0:T(8,128)}, bf16[2,128,16,64]{1,3,2,0:T(8,128)(2,1)S(1)}, pred[2,128,128]{2,1,0:T(8,128)(4,1)}, f32[2,128,1...) while((s32[]{:T(128)}, f32[2,128,16,64]{1,3,2,0:T(8,128)}, ...), condition=%wide.region_4.5_spmd, body=%wide.region_3.4_spmd.sunk | while | flops 71172096 | bytes 2507877 | solution.py:46
  133.8 9.1 %while.41 = (s32[]{:T(128)}, f32[2,128,16,64]{1,3,2,0:T(8,128)}, bf16[2,128,16,64]{1,3,2,0:T(8,128)(2,1)}, pred[2,128,128]{2,1,0:T(8,128)(4,1)S(1)}, f32[2,128,1...) while((s32[]{:T(128)}, f32[2,128,16,64]{1,3,2,0:T(8,128)}, ...), condition=%wide.region_7.8_spmd, body=%wide.region_6.7_spmd.sunk | while | flops 71172096 | bytes 2508385 | solution.py:46
  136.1 2.3 fusion.221
  140.7 2.3 fusion.221
  146.3 5.3 %while.42 = (s32[]{:T(128)}, f32[2,128,16,64]{1,3,2,0:T(8,128)}, bf16[2,128,16,64]{1,3,2,0:T(8,128)(2,1)S(1)}, pred[2,128,128]{2,1,0:T(8,128)(4,1)S(1)}, f32[2,1...) while((s32[]{:T(128)}, f32[2,128,16,64]{1,3,2,0:T(8,128)}, ...), condition=%wide.region_10.11_spmd, body=%wide.region_9.10_spmd.sunk | while | flops 71172096 | bytes 2507877 | solution.py:46
  156.7 10.6 %while.43 = (s32[]{:T(128)}, f32[2,128,16,64]{1,3,2,0:T(8,128)}, bf16[2,128,16,64]{1,3,2,0:T(8,128)(2,1)}, pred[2,128,128]{2,1,0:T(8,128)(4,1)}, f32[2,128,16]{1...) while((s32[]{:T(128)}, f32[2,128,16,64]{1,3,2,0:T(8,128)}, ...), condition=%wide.region_13.14_spmd, body=%wide.region_12.13_spmd.sunk | while | flops 71172096 | bytes 2508385 | solution.py:46
  159.6 2.3 fusion.231
  164.8 2.4 fusion.231
  179.5 2.6 bitcast_reduce_fusion
  182.2 1.8 fusion.85
  184.9 82.7 %all-gather.4.cloned.1.call-done = bf16[512,8192]{0,1:T(8,128)(2,1)} async-done(((bf16[512,2048]{0,1:T(8,128)(2,1)}), bf16[512,8192]{0,1:T(8,128)(2,1)}) %all-gather.4.cloned.1.call-update) | async-done | bytes 8388624 | tf_op jit(solution)/shard_map/all_gather | solution.py:169
  267.6 76.5 %all-gather.6.cloned.1.call-done = bf16[8192,1024]{1,0:T(8,128)(2,1)} async-done(((bf16[256,1024]{1,0:T(8,128)(2,1)}), bf16[8192,1024]{1,0:T(8,128)(2,1)}) %all-gather.6.cloned.1.call-update) | async-done | bytes 16777232 | tf_op jit(solution)/shard_map/all_gather | solution.py:168
  344.1 14.8 %add_convert_fusion = bf16[512,1024]{1,0:T(8,128)(2,1)S(1)} fusion(bf16[512,1024]{1,0:T(8,128)(2,1)S(1)} %copy-done.37, bf16[512,8192]{0,1:T(8,128)(2,1)} %all-gather.4.cloned.1.call-done, bf16[8192,1024]{1,0:T(8,128)(2,1)} %all-gather.6.cloned.1.call-done), kind=kOutput, calls=%fused_computation.111 | convolution fusion | flops 8592556032 | bytes 27262976 | tf_op jit(solution)/shard_map/dot_general | solution.py:170
  359.3 55.9 %all-gather = bf16[128,2,1024]{2,1,0:T(2,128)(2,1)S(1)} all-gather(bf16[1,2,1024]{2,1,0:T(2,128)(2,1)S(1)} %fusion.111), channel_id=1, replica_groups=mesh['req'=32,'seq'=4] {'req','seq'}, dimensions={0}, use_global_device_ids=true | all-gather | bytes 528384 | tf_op jit(solution)/shard_map/all_gather | solution.py:177
  416.9 2.7 fusion.118
  (206 shorter events, 73.9 us)
Async XLA Ops:
  7.2 176.9 %copy-start = (bf16[256,4096]{1,0:T(8,128)(2,1)S(1)}, bf16[256,4096]{1,0:T(8,128)(2,1)}, u32[]{:S(2)}) copy-start(bf16[256,4096]{1,0:T(8,128)(2,1)} %param.30) | copy-start | bytes 6291460
  12.6 7.5 %copy-start.23 = (bf16[128,128]{1,0:T(8,128)(2,1)S(1)}, bf16[128,128]{1,0:T(8,128)(2,1)}, u32[]{:S(2)}) copy-start(bf16[128,128]{1,0:T(8,128)(2,1)} %param.24) | copy-start | bytes 98308
  25.7 5.2 %copy-start.38 = (s32[1,2]{1,0:T(1,128)S(1)}, s32[1,2]{1,0:T(1,128)}, u32[]{:S(2)}) copy-start(s32[1,2]{1,0:T(1,128)} %param.33) | copy-start | bytes 28
  25.7 9.1 %copy-start.39 = (f32[128]{0:T(128)S(1)}, f32[128]{0:T(128)}, u32[]{:S(2)}) copy-start(f32[128]{0:T(128)} %param.25) | copy-start | bytes 1540
  25.7 9.2 %copy-start.40 = (f32[128]{0:T(128)S(1)}, f32[128]{0:T(128)}, u32[]{:S(2)}) copy-start(f32[128]{0:T(128)} %param.27) | copy-start | bytes 1540
  25.7 10.0 %copy-start.41 = (f32[128]{0:T(128)S(1)}, f32[128]{0:T(128)}, u32[]{:S(2)}) copy-start(f32[128]{0:T(128)} %param.26) | copy-start | bytes 1540
  25.7 60.3 %all-to-all-start = ((bf16[128,4,4640]{0,2,1:T(8,128)(2,1)}), bf16[128,4,4640]{0,2,1:T(8,128)(2,1)}, u32[]{:S(2)}, u32[]{:S(2)}) async-start(bf16[128,4,4640]{0,2,1:T(8,128)(2,1)} %constant_dynamic-update-slice_fusion), calls=%async_computation | async-start | bytes 9502720 | tf_op jit(solution)/shard_map/all_to_all | solution.py:123
  30.9 236.8 %all-gather.4.cloned.1.call-start = ((), (), s32[]{:S(2)}) async-start(), calls=%async_computation.1 | async-start | bytes 10485760 | tf_op jit(solution)/shard_map/all_gather | solution.py:169
  31.1 73.3 %copy-start.34 = (s32[2,1]{0,1:T(1,128)}, s32[2,1]{0,1:T(1,128)S(1)}, u32[]{:S(2)}) copy-start(s32[2,1]{0,1:T(1,128)S(1)} %reduce-window.7) | copy-start | bytes 28
  106.2 24.7 %copy-start.8 = (bf16[128,256]{0,1:T(8,128)(2,1)}, bf16[128,256]{0,1:T(8,128)(2,1)S(1)}, u32[]{:S(2)}) copy-start(bf16[128,256]{0,1:T(8,128)(2,1)S(1)} %get-tuple-element.281) | copy-start | bytes 196612
  106.2 38.1 %copy-start.10 = (bf16[128,256]{0,1:T(8,128)(2,1)}, bf16[128,256]{0,1:T(8,128)(2,1)S(1)}, u32[]{:S(2)}) copy-start(bf16[128,256]{0,1:T(8,128)(2,1)S(1)} %get-tuple-element.278) | copy-start | bytes 196612
  108.1 11.0 %copy-start.15 = (f32[512,32]{0,1:T(8,128)}, f32[512,32]{0,1:T(8,128)S(1)}, u32[]{:S(2)}) copy-start(f32[512,32]{0,1:T(8,128)S(1)} %compare_select_fusion) | copy-start | bytes 196612
  133.8 12.4 %copy-start.17 = (f32[128,32]{0,1:T(8,128)S(1)}, f32[128,32]{0,1:T(8,128)}, u32[]{:S(2)}) copy-start(f32[128,32]{0,1:T(8,128)} %copy.360) | copy-start | bytes 49156
  146.3 5.3 %copy-start.36 = (f32[32]{0:T(128)S(1)}, f32[32]{0:T(128)}, u32[]{:S(2)}) copy-start(f32[32]{0:T(128)} %get-tuple-element.325) | copy-start | bytes 388
  146.3 5.9 %copy-start.22 = (f32[128,32]{0,1:T(8,128)S(1)}, f32[128,32]{0,1:T(8,128)}, u32[]{:S(2)}) copy-start(f32[128,32]{0,1:T(8,128)} %get-tuple-element.289) | copy-start | bytes 49156
  167.2 7.4 %copy-start.9 = (bf16[128,256]{0,1:T(8,128)(2,1)S(1)}, bf16[128,256]{0,1:T(8,128)(2,1)}, u32[]{:S(2)}) copy-start(bf16[128,256]{0,1:T(8,128)(2,1)} %copy-done.8) | copy-start | bytes 196612
  169.9 5.0 %copy-start.12 = (bf16[128,256]{0,1:T(8,128)(2,1)S(1)}, bf16[128,256]{0,1:T(8,128)(2,1)}, u32[]{:S(2)}) copy-start(bf16[128,256]{0,1:T(8,128)(2,1)} %get-tuple-element.280) | copy-start | bytes 196612
  169.9 5.0 %copy-start.20 = (f32[128,32]{0,1:T(8,128)S(1)}, f32[128,32]{0,1:T(8,128)}, u32[]{:S(2)}) copy-start(f32[128,32]{0,1:T(8,128)} %get-tuple-element.300) | copy-start | bytes 49156
  169.9 5.3 %copy-start.32 = (f32[2,16]{1,0:T(2,128)S(1)}, f32[2,16]{1,0:T(2,128)}, u32[]{:S(2)}) copy-start(f32[2,16]{1,0:T(2,128)} %mul.517) | copy-start | bytes 388
  171.5 3.4 copy-start.2
  182.1 162.0 %copy-start.37 = (bf16[512,1024]{1,0:T(8,128)(2,1)S(1)}, bf16[512,1024]{1,0:T(8,128)(2,1)}, u32[]{:S(2)}) copy-start(bf16[512,1024]{1,0:T(8,128)(2,1)} %param.29) | copy-start | bytes 3145732
  184.0 160.1 %all-gather.6.cloned.1.call-start = ((), (), s32[]{:S(2)}) async-start(), calls=%async_computation.2 | async-start | bytes 17301504 | tf_op jit(solution)/shard_map/all_gather | solution.py:168
  359.0 57.7 %copy-start.13 = (bf16[512,1024]{1,0:T(8,128)(2,1)}, bf16[512,1024]{1,0:T(8,128)(2,1)S(1)}, u32[]{:S(2)}) copy-start(bf16[512,1024]{1,0:T(8,128)(2,1)S(1)} %add_convert_fusion) | copy-start | bytes 3145732
  359.0 57.9 %copy-start.24 = (f32[4096]{0:T(1024)S(1)}, f32[4096]{0:T(1024)}, u32[]{:S(2)}) copy-start(f32[4096]{0:T(1024)} %param.31) | copy-start | bytes 49156
  (22 other events, 31.8 us)
Sparse Core Ops, SparseCore 0:
  184.1 83.4 all-gather.3
  270.5 73.5 all-gather.5
where the time goes:
time: 429 us; the launch traced here: 426 us
  waiting for transfers between devices  205 us (48%)
  local copies, waits for them, and re-layouts  71.9 us (17%)
  blocking collectives  55.9 us (13%)
  matrix products  50.2 us (12%)
  other arithmetic  20.6 us (5%)
  between operations  17.7 us (4%)
  starting transfers between devices  5.2 us (1%)
    all_gather x1, waiting for transfers between devices, on_device(): gated_all = lax.all_gather(gated, 'seq', axis=1, tiled=True)  82.7 us
    all_gather x1, waiting for transfers between devices, on_device(): w_full = lax.all_gather(w_cols, 'req', axis=0, tiled=True)  76.5 us
    all_gather x1, blocking collectives, on_device(): collected = lax.all_gather(picked_rows, ('req', 'seq'), axis=0, tiled=True)  55.9 us
    all_to_all x1, waiting for transfers between devices, on_device(): lax.all_to_all(packed, 'seq', split_axis=1, concat_axis=0, tiled=True)  45.8 us
    unnamed x93, local copies, waits for them, and re-layouts  18.8 us
    all_to_all x1, local copies, waits for them, and re-layouts, on_device(): lax.all_to_all(packed, 'seq', split_axis=1, concat_axis=0, tiled=True)  18.4 us
    dot_general x8, matrix products, group_inner(): jnp.einsum('tsk,skp->tkp', lower, x_g, preferred_element_type=jnp.float32)  14.9 us
    dot_general x1, matrix products, on_device(): jnp.dot(gated_all, w_full, preferred_element_type=jnp.float32)  14.8 us
  transfers between devices with their start and end apart: 3, of which 3 were waited for; matrix products, arithmetic and copies ran while one was open for 2% of the time, Pallas kernels for 0%

commit v1 on v0

--- a/solution.py
+++ b/solution.py
@@ -7,6 +7,28 @@
 HEAD_DIM = 64
 NGROUPS = 8
 STATE = 128
+
+
+def in_order(pieces, dim):
+    pieces = jnp.moveaxis(pieces, 0, dim)
+    shape = pieces.shape
+    return pieces.reshape(*shape[:dim], shape[dim] * shape[dim + 1], *shape[dim + 2 :])
+
+
+def gather_around(value, axis, dim):
+    devices = lax.axis_size(axis)
+    pairs = [(i, (i + 1) % devices) for i in range(devices)]
+    back = [(b, a) for a, b in pairs]
+    lower, upper = ([], [])
+    for step in range(devices - 1):
+        if step % 2 == 0:
+            lower.append(lax.ppermute(lower[-1] if lower else value, axis, pairs))
+        else:
+            upper.append(lax.ppermute(upper[-1] if upper else value, axis, back))
+    pieces = jnp.stack([*lower[::-1], value, *upper])
+    shift = lax.axis_index(axis) - len(lower)
+    pieces = pieces[(jnp.arange(devices) - shift) % devices]
+    return in_order(pieces, dim)
 
 
 def split_halves(value):
@@ -166,7 +188,7 @@
     width = resid.shape[1]
     w_cols = lax.dynamic_slice_in_dim(w_out, place * width, width, axis=1)
     w_full = lax.all_gather(w_cols, "req", axis=0, tiled=True)
-    gated_all = lax.all_gather(gated, "seq", axis=1, tiled=True)
+    gated_all = gather_around(gated, "seq", 1)
     mixer = jnp.dot(gated_all, w_full, preferred_element_type=jnp.float32).astype(jnp.bfloat16)
     layer_out = (resid.astype(jnp.float32) + mixer.astype(jnp.float32)).astype(jnp.bfloat16)
     group_pos = jnp.arange(group_rows, dtype=jnp.int32)

time: 429 us -> 390 us (0.909)
  waiting for transfers between devices: 205 us -> 139 us
  matrix products: 50.2 us -> 66.7 us
  local copies, waits for them, and re-layouts: 71.9 us -> 77 us
    ppermute x0 -> x3, waiting for transfers between devices: none -> 91.9 us  [the longest x2 91.9 us: gather_around(): lower.append(lax.ppermute(lower[-1] if lower else value, axis, pairs))]
    all_gather x1 -> x0, waiting for transfers between devices: 82.7 us -> none  [on_device(): gated_all = lax.all_gather(gated, 'seq', axis=1, tiled=True)]
    all_gather x1, waiting for transfers between devices: 76.5 us -> 0.01 us  [on_device(): w_full = lax.all_gather(w_cols, 'req', axis=0, tiled=True)]
    gather x0 -> x3, local copies, waits for them, and re-layouts: none -> 13.6 us  [gather_around(): pieces = pieces[(jnp.arange(devices) - shift) % devices]]
    unnamed x0 -> x1, other arithmetic: none -> 7.36 us
    dot_general x3, matrix products: 1.19 us -> 8 us  [carry_term(): jnp.einsum('tgn,gkpn->tgkp', cmat, lower, preferred_element_type=jnp.floa...]
    dot_general x4, matrix products: 1.19 us -> 6.59 us  [carry_term(): jnp.einsum('tgn,gkpn->tgkp', cmat, upper, preferred_element_type=jnp.floa...]
    unnamed x93 -> x99, local copies, waits for them, and re-layouts: 18.8 us -> 19.6 us
  transfers between devices with their start and end apart: 3 -> 5, of which waited for: 3 -> 3; matrix products, arithmetic and copies ran while one was open for 2% -> 36% of each run, Pallas kernels for 0% -> 0%
where the time goes in v1:
time: 390 us; the launch traced here: 387 us
  waiting for transfers between devices  139 us (36%)
  local copies, waits for them, and re-layouts  77 us (20%)
  matrix products  66.7 us (17%)
  blocking collectives  56.4 us (14%)
  other arithmetic  21.7 us (6%)
  between operations  17.9 us (5%)
  starting transfers between devices  8.45 us (2%)
    ppermute x2, waiting for transfers between devices, gather_around(): lower.append(lax.ppermute(lower[-1] if lower else value, axis, pairs))  91.9 us
    all_gather x1, blocking collectives, on_device(): collected = lax.all_gather(picked_rows, ('req', 'seq'), axis=0, tiled=True)  56.4 us
    all_to_all x1, waiting for transfers between devices, on_device(): lax.all_to_all(packed, 'seq', split_axis=1, concat_axis=0, tiled=True)  46.8 us
    unnamed x99, local copies, waits for them, and re-layouts  19.6 us
    dot_general x8, matrix products, group_inner(): jnp.einsum('tsk,skp->tkp', lower, x_g, preferred_element_type=jnp.float32)  18.9 us
    all_to_all x1, local copies, waits for them, and re-layouts, on_device(): lax.all_to_all(packed, 'seq', split_axis=1, concat_axis=0, tiled=True)  18.4 us
    dot_general x1, matrix products, on_device(): jnp.dot(gated_all, w_full, preferred_element_type=jnp.float32)  14.9 us
    gather x3, local copies, waits for them, and re-layouts, gather_around(): pieces = pieces[(jnp.arange(devices) - shift) % devices]  13.6 us
  transfers between devices with their start and end apart: 5, of which 3 were waited for; matrix products, arithmetic and copies ran while one was open for 36% of the time, Pallas kernels for 0%

profile of v1, /device:TPU:0, one launch (start us, length us, event | category | flops | bytes accessed | tf_op | source)
XLA Modules:
  0.0 387.2 jit_solution(12070511470077543668)
XLA Ops:
  10.9 4.1 %copy.344 = bf16[128,8192]{0,1:T(8,128)(2,1)} copy(bf16[128,8192]{1,0:T(8,128)(2,1)} %param.21) | data formatting | bytes 4194304 | tf_op args[0]
  15.0 3.2 copy.345
  18.5 3.3 constant_dynamic-update-slice_fusion.4
  25.7 5.1 %all-to-all-start = ((bf16[128,4,4640]{0,2,1:T(8,128)(2,1)}), bf16[128,4,4640]{0,2,1:T(8,128)(2,1)}, u32[]{:S(2)}, u32[]{:S(2)}) async-start(bf16[128,4,4640]{0,2,1:T(8,128)(2,1)} %constant_dynamic-update-slice_fusion), calls=%async_computation | async-start | bytes 9502720 | tf_op jit(solution)/shard_map/all_to_all | solution.py:145
  39.2 46.8 %all-to-all-done = bf16[128,4,4640]{0,2,1:T(8,128)(2,1)} async-done(((bf16[128,4,4640]{0,2,1:T(8,128)(2,1)}), bf16[128,4,4640]{0,2,1:T(8,128)(2,1)}, u32[]{:S(2)}, u32[]{:S(2)}) %all-to-all-start) | async-done | bytes 4751392 | tf_op jit(solution)/shard_map/all_to_all | solution.py:145
  86.0 18.4 %copy.349 = bf16[4,128,1,4640]{1,0,3,2:T(4,128)(2,1)S(1)} copy(bf16[4,128,1,4640]{1,3,0,2:T(8,128)(2,1)} %bitcast.34) | data formatting | bytes 9502720 | tf_op jit(solution)/shard_map/all_to_all | solution.py:145
  126.0 12.2 %while.40 = (s32[]{:T(128)}, f32[2,128,16,64]{1,3,2,0:T(8,128)}, bf16[2,128,16,64]{1,3,2,0:T(8,128)(2,1)}, pred[2,128,128]{2,1,0:T(8,128)(4,1)}, f32[2,128,16]{1...) while((s32[]{:T(128)}, f32[2,128,16,64]{1,3,2,0:T(8,128)}, ...), condition=%wide.region_4.5_spmd, body=%wide.region_3.4_spmd.sunk | while | flops 71172096 | bytes 2508385 | solution.py:68
  138.3 2.8 fusion.89
  143.6 10.6 %while.41 = (s32[]{:T(128)}, f32[2,128,16,64]{1,3,2,0:T(8,128)}, bf16[2,128,16,64]{1,3,2,0:T(8,128)(2,1)}, pred[2,128,128]{2,1,0:T(8,128)(4,1)}, f32[2,128,16]{1...) while((s32[]{:T(128)}, f32[2,128,16,64]{1,3,2,0:T(8,128)}, ...), condition=%wide.region_7.8_spmd, body=%wide.region_6.7_spmd.sunk | while | flops 71172096 | bytes 2508385 | solution.py:68
  154.2 3.1 fusion.103
  158.5 8.1 %while.42 = (s32[]{:T(128)}, f32[2,128,16,64]{1,3,2,0:T(8,128)}, bf16[2,128,16,64]{1,3,2,0:T(8,128)(2,1)}, pred[2,128,128]{2,1,0:T(8,128)(4,1)S(1)}, f32[2,128,1...) while((s32[]{:T(128)}, f32[2,128,16,64]{1,3,2,0:T(8,128)}, ...), condition=%wide.region_10.11_spmd, body=%wide.region_9.10_spmd.sunk | while | flops 71172096 | bytes 2508385 | solution.py:68
  166.6 2.7 fusion.98
  170.6 7.8 %while.43 = (s32[]{:T(128)}, f32[2,128,16,64]{1,3,2,0:T(8,128)}, bf16[2,128,16,64]{1,3,2,0:T(8,128)(2,1)}, pred[2,128,128]{2,1,0:T(8,128)(4,1)S(1)}, f32[2,128,1...) while((s32[]{:T(128)}, f32[2,128,16,64]{1,3,2,0:T(8,128)}, ...), condition=%wide.region_13.14_spmd, body=%wide.region_12.13_spmd.sunk | while | flops 71172096 | bytes 2508385 | solution.py:68
  181.1 2.6 bitcast_reduce_fusion
  187.5 44.7 %collective-permute-done = bf16[512,2048]{0,1:T(8,128)(2,1)} collective-permute-done((bf16[512,2048]{0,1:T(8,128)(2,1)S(1)}, bf16[512,2048]{0,1:T(8,128)(2,1)}, u32[]{:S(2)}, u32[]{:S(2)}) %collective-permute-start) | collective-permute-done | bytes 2097184 | tf_op jit(solution)/shard_map/ppermute | solution.py:25
  232.2 47.2 %collective-permute-done.1 = bf16[512,2048]{0,1:T(8,128)(2,1)} collective-permute-done((bf16[512,2048]{0,1:T(8,128)(2,1)}, bf16[512,2048]{0,1:T(8,128)(2,1)}, u32[]{:S(2)}, u32[]{:S(2)}) %collective-permute-start.1) | collective-permute-done | bytes 2097184 | tf_op jit(solution)/shard_map/ppermute | solution.py:25
  279.4 3.8 pad_maximum_fusion
  283.2 3.6 fusion.158
  286.9 5.0 %gather_fusion = bf16[4,512,1024]{1,2,0:T(8,128)(2,1)} fusion(bf16[4,512,1024]{1,2,0:T(8,128)(2,1)} %get-tuple-element.275, s32[1024]{0:T(1024)S(1)} %pad_clamp_fusion), kind=kCustom, calls=%fused_computation | custom fusion | bytes 8388624 | tf_op jit(solution)/shard_map/gather | solution.py:30
  291.9 5.0 %gather_fusion.1 = bf16[4,512,1024]{1,2,0:T(8,128)(2,1)} fusion(bf16[4,512,1024]{1,2,0:T(8,128)(2,1)} %get-tuple-element.276, s32[1024]{0:T(1024)S(1)} %pad_clamp_fusion), kind=kCustom, calls=%fused_computation.1 | custom fusion | bytes 8388624 | tf_op jit(solution)/shard_map/gather | solution.py:30
  296.9 7.4 %pad_maximum_fusion.1 = bf16[4,512,2048]{1,2,0:T(8,128)(2,1)} fusion(bf16[4,512,1024]{1,2,0:T(8,128)(2,1)} %gather_fusion.1, bf16[4,512,1024]{1,2,0:T(8,128)(2,1)} %gather_fusion), kind=kLoop, calls=%fused_computation.103 | loop fusion | flops 16777216 | bytes 16777216
  304.2 14.9 %add_convert_fusion = bf16[512,1024]{1,0:T(8,128)(2,1)S(1)} fusion(bf16[512,1024]{1,0:T(8,128)(2,1)S(1)} %copy-done.40, bf16[512,8192]{0,1:T(8,128)(2,1)} %bitcast.334, bf16[8192,1024]{1,0:T(8,128)(2,1)} %all-gather.3.cloned.1.call-done), kind=kOutput, calls=%fused_computation.115 | convolution fusion | flops 8592556032 | bytes 27262976 | tf_op jit(solution)/shard_map/dot_general | solution.py:192
  319.4 56.4 %all-gather = bf16[128,2,1024]{2,1,0:T(2,128)(2,1)S(1)} all-gather(bf16[1,2,1024]{2,1,0:T(2,128)(2,1)S(1)} %fusion.111), channel_id=1, replica_groups=mesh['req'=32,'seq'=4] {'req','seq'}, dimensions={0}, use_global_device_ids=true | all-gather | bytes 528384 | tf_op jit(solution)/shard_map/all_gather | solution.py:199
  377.6 2.7 fusion.118
  (222 shorter events, 86.1 us)
Async XLA Ops:
  7.2 297.0 %all-gather.3.cloned.1.call-start = ((), (), s32[]{:S(2)}) async-start(), calls=%async_computation.1 | async-start | bytes 17301504 | tf_op jit(solution)/shard_map/all_gather | solution.py:190
  25.7 9.2 %copy-start.42 = (f32[128]{0:T(128)S(1)}, f32[128]{0:T(128)}, u32[]{:S(2)}) copy-start(f32[128]{0:T(128)} %param.25) | copy-start | bytes 1540
  25.7 9.3 %copy-start.43 = (f32[128]{0:T(128)S(1)}, f32[128]{0:T(128)}, u32[]{:S(2)}) copy-start(f32[128]{0:T(128)} %param.27) | copy-start | bytes 1540
  25.7 10.0 %copy-start.44 = (f32[128]{0:T(128)S(1)}, f32[128]{0:T(128)}, u32[]{:S(2)}) copy-start(f32[128]{0:T(128)} %param.26) | copy-start | bytes 1540
  25.7 60.3 %all-to-all-start = ((bf16[128,4,4640]{0,2,1:T(8,128)(2,1)}), bf16[128,4,4640]{0,2,1:T(8,128)(2,1)}, u32[]{:S(2)}, u32[]{:S(2)}) async-start(bf16[128,4,4640]{0,2,1:T(8,128)(2,1)} %constant_dynamic-update-slice_fusion), calls=%async_computation | async-start | bytes 9502720 | tf_op jit(solution)/shard_map/all_to_all | solution.py:145
  35.8 76.8 %copy-start.32 = (f32[128]{0:T(128)}, f32[128]{0:T(128)S(1)}, u32[]{:S(2)}) copy-start(f32[128]{0:T(128)S(1)} %get-tuple-element.320) | copy-start | bytes 1540
  35.8 76.8 %copy-start.34 = (f32[128]{0:T(128)}, f32[128]{0:T(128)S(1)}, u32[]{:S(2)}) copy-start(f32[128]{0:T(128)S(1)} %get-tuple-element.321) | copy-start | bytes 1540
  35.8 76.8 %copy-start.35 = (f32[128]{0:T(128)}, f32[128]{0:T(128)S(1)}, u32[]{:S(2)}) copy-start(f32[128]{0:T(128)S(1)} %get-tuple-element.322) | copy-start | bytes 1540
  35.8 76.8 %copy-start.36 = (f32[128]{0:T(128)}, f32[128]{0:T(128)S(1)}, u32[]{:S(2)}) copy-start(f32[128]{0:T(128)S(1)} %get-tuple-element.323) | copy-start | bytes 1540
  108.4 10.4 %copy-start.19 = (f32[128,32]{0,1:T(8,128)}, f32[128,32]{0,1:T(8,128)S(1)}, u32[]{:S(2)}) copy-start(f32[128,32]{0,1:T(8,128)S(1)} %copy.356) | copy-start | bytes 49156
  108.6 10.1 %copy-start.17 = (f32[128,32]{0,1:T(8,128)}, f32[128,32]{0,1:T(8,128)S(1)}, u32[]{:S(2)}) copy-start(f32[128,32]{0,1:T(8,128)S(1)} %copy.365) | copy-start | bytes 49156
  114.4 8.6 %copy-start.10 = (bf16[128,256]{0,1:T(8,128)(2,1)}, bf16[128,256]{0,1:T(8,128)(2,1)S(1)}, u32[]{:S(2)}) copy-start(bf16[128,256]{0,1:T(8,128)(2,1)S(1)} %get-tuple-element.279) | copy-start | bytes 196612
  143.6 10.6 %copy-start.25 = (f32[128,2,16]{0,2,1:T(8,128)S(1)}, f32[128,2,16]{0,2,1:T(8,128)}, u32[]{:S(2)}) copy-start(f32[128,2,16]{0,2,1:T(8,128)} %get-tuple-element.325) | copy-start | bytes 49156
  158.5 8.1 %copy-start.9 = (f32[2,16,64,128]{3,2,1,0:T(8,128)S(1)}, f32[2,16,64,128]{3,2,1,0:T(8,128)}, u32[]{:S(2)}) copy-start(f32[2,16,64,128]{3,2,1,0:T(8,128)} %fusion.140) | copy-start | bytes 3145732
  158.5 8.1 %copy-start.13 = (bf16[128,256]{0,1:T(8,128)(2,1)S(1)}, bf16[128,256]{0,1:T(8,128)(2,1)}, u32[]{:S(2)}) copy-start(bf16[128,256]{0,1:T(8,128)(2,1)} %copy-done.12) | copy-start | bytes 196612
  158.5 8.1 %copy-start.24 = (f32[128,2,16]{0,2,1:T(8,128)S(1)}, f32[128,2,16]{0,2,1:T(8,128)}, u32[]{:S(2)}) copy-start(f32[128,2,16]{0,2,1:T(8,128)} %get-tuple-element.324) | copy-start | bytes 49156
  170.6 7.9 %copy-start.31 = (f32[2,16]{1,0:T(2,128)S(1)}, f32[2,16]{1,0:T(2,128)}, u32[]{:S(2)}) copy-start(f32[2,16]{1,0:T(2,128)} %mul.481) | copy-start | bytes 388
  183.7 48.5 %copy-start.39 = (s32[2,1]{0,1:T(1,128)S(1)}, s32[2,1]{0,1:T(1,128)}, u32[]{:S(2)}) copy-start(s32[2,1]{0,1:T(1,128)} %copy-done.38) | copy-start | bytes 28
  184.2 48.0 %collective-permute-start = (bf16[512,2048]{0,1:T(8,128)(2,1)S(1)}, bf16[512,2048]{0,1:T(8,128)(2,1)}, u32[]{:S(2)}, u32[]{:S(2)}) collective-permute-start(bf16[512,2048]{0,1:T(8,128)(2,1)S(1)} %fusion.85), channel_id=1, source_target_pairs={{0,1},{1,2},{2,3},{3,0},{4,5},{5,6},{6,7},{7,4},{8,9},{9,10},{10,1... | collective-permute-start | bytes 6291464 | tf_op jit(solution)/shard_map/ppermute | solution.py:25
  184.9 47.3 %collective-permute-start.2 = (bf16[512,2048]{0,1:T(8,128)(2,1)S(1)}, bf16[512,2048]{0,1:T(8,128)(2,1)}, u32[]{:S(2)}, u32[]{:S(2)}) collective-permute-start(bf16[512,2048]{0,1:T(8,128)(2,1)S(1)} %fusion.85), channel_id=1, source_target_pairs={{1,0},{2,1},{3,2},{0,3},{5,4},{6,5},{7,6},{4,7},{9,8},{10,9},{11,1... | collective-permute-start | bytes 6291464 | tf_op jit(solution)/shard_map/ppermute | solution.py:27
  232.1 47.3 %collective-permute-start.1 = (bf16[512,2048]{0,1:T(8,128)(2,1)}, bf16[512,2048]{0,1:T(8,128)(2,1)}, u32[]{:S(2)}, u32[]{:S(2)}) collective-permute-start(bf16[512,2048]{0,1:T(8,128)(2,1)} %collective-permute-done), channel_id=1, source_target_pairs={{0,1},{1,2},{2,3},{3,0},{4,5},{5,6},{6,7},{7,4},{8,9},{9,10},{10,1... | collective-permute-start | bytes 6291464 | tf_op jit(solution)/shard_map/ppermute | solution.py:25
  319.1 58.3 %copy-start.15 = (bf16[512,1024]{1,0:T(8,128)(2,1)}, bf16[512,1024]{1,0:T(8,128)(2,1)S(1)}, u32[]{:S(2)}) copy-start(bf16[512,1024]{1,0:T(8,128)(2,1)S(1)} %add_convert_fusion) | copy-start | bytes 3145732
  319.1 58.5 %copy-start.30 = (f32[4096]{0:T(1024)S(1)}, f32[4096]{0:T(1024)}, u32[]{:S(2)}) copy-start(f32[4096]{0:T(1024)} %param.31) | copy-start | bytes 49156
  319.1 61.2 %copy-start.1 = (bf16[256,4096]{1,0:T(8,128)(2,1)S(1)}, bf16[256,4096]{1,0:T(8,128)(2,1)}, u32[]{:S(2)}) copy-start(bf16[256,4096]{1,0:T(8,128)(2,1)} %param.30) | copy-start | bytes 6291460
  (27 other events, 116.7 us)
Sparse Core Ops, SparseCore 0:
  10.2 75.1 all-gather.2
